TPU v7x, 256 devices: a whole 4x4x8 slice. The times are simulated.
256 devices in a mesh: heads: 4 (over x), seq: 64 (over z, y, core).
Axes of the slice: x: 4, y: 4, z: 8, core: 2. Of those that a mesh axis runs over, the one named last changes fastest.
Arguments:
- queries: bfloat16 [32768, 2048], P('seq', 'heads'), may hold values from -64 to 64
- keys: bfloat16 [32768, 512], P('seq', 'heads'), may hold values from -6 to 6
- values: bfloat16 [32768, 512], P('seq', 'heads'), may hold values from -6 to 6
- vertical: int32 [16, 16], replicated, may hold values from 0 to 511, as said below
- slash: int32 [16, 8], replicated, may hold values from 0 to 15, as said below
- out_weight: bfloat16 [2048, 4096], P('heads'), may hold values from -0.25 to 0.25
Outputs:
- layer_out: bfloat16 [32768, 4096], P('seq', 'heads')
Inputs may be any that keep to these rules, and one draw needn't show every extreme that they name: `vertical`: each row lists 16 distinct blocks; the four rows of one KV head (rows 4g to 4g+3) list 64 distinct blocks in all; at most 2 of those lie within blocks k * 8 to (k + 1) * 8 - 1 for any k, and in every draw some k reaches 2. `slash`: each row lists 8 distinct offsets, 0 among them; some row holds 15 in every draw.
All inputs are finite; a program needn't handle non-finite values.
Results may differ from a plain program's by a relative error of at most 0.0095.
Values may be sent and summed in bfloat16 or wider, within the bound.
No kernel may reach another device: no remote copies, remote signals or barrier semaphores. Data moves between devices by JAX's collectives and lax.ppermute only.
A program may use at most 128 MiB of HBM per device.

v0:
```python
import math
import jax
import jax.numpy as jnp
import numpy as np
from jax import lax
from jax.sharding import Mesh
from jax.sharding import PartitionSpec as P

HEAD_SIZE = 128
BLOCK_TOKENS = 64
SEQ = ("z", "y", "core")


def shift(block, axis, size, distance):
    route = [(i, i + distance) for i in range(size) if 0 <= i + distance < size]
    return lax.ppermute(block, axis, route)


def ring(block, axis, size, distance):
    return lax.ppermute(block, axis, [(i, (i + distance) % size) for i in range(size)])


def spread(table, rows, cols):
    return jnp.repeat(jnp.repeat(table, rows, axis=-2), cols, axis=-1)


def make_local(sizes):
    heads_n, z_n, y_n, core_n = sizes
    cycle_size = z_n * y_n * core_n

    def local(queries, keys, values, vertical, slash, out_weight):
        head_dim = HEAD_SIZE
        local_heads = queries.shape[1] // head_dim
        token_count = queries.shape[0]
        block_count = token_count // BLOCK_TOKENS
        score_scale = 1.0 / math.sqrt(head_dim)
        kv_group = lax.axis_index("heads")
        core = lax.axis_index("core")
        cycle_index = lax.axis_index(SEQ)
        vert_group = lax.dynamic_slice_in_dim(vertical, kv_group * local_heads, local_heads, 0)
        slash_group = lax.dynamic_slice_in_dim(slash, kv_group * local_heads, local_heads, 0)
        union_list = vert_group.reshape(-1)
        listed_count = union_list.shape[0]
        owner_dev = union_list // block_count
        within_dev = union_list % block_count
        paired = jnp.stack([keys, values]).reshape(2, block_count, BLOCK_TOKENS, head_dim)
        owned_here = owner_dev == cycle_index
        capacity = min(block_count, max(2, 2 * listed_count // cycle_size))
        positions = jnp.arange(listed_count)
        same_owner = (owner_dev[:, None] == owner_dev[None, :]) & (
            positions[None, :] < positions[:, None]
        )
        slot_index = jnp.sum(same_owner.astype(jnp.int32), axis=1)
        selector = owned_here[None, :] & (slot_index[None, :] == jnp.arange(capacity)[:, None])
        picked = jnp.sum(jnp.where(selector, within_dev[None, :], 0), axis=1)
        outgoing = paired[:, picked].reshape(2, capacity * BLOCK_TOKENS, head_dim)
        arrived = lax.all_gather(outgoing, SEQ, axis=1, tiled=True)
        rows_total, width = out_weight.shape
        col_width = width // heads_n
        half_rows = rows_total // core_n
        fetched = []
        for distance in range(1, heads_n):
            dest_cols = (kv_group + distance) % heads_n * col_width
            piece = lax.dynamic_slice(
                out_weight, (core * half_rows, dest_cols), (half_rows, col_width)
            )
            fetched.append(ring(piece, "heads", heads_n, distance))
        fetched = jnp.stack(fetched)
        sibling_w = ring(fetched, "core", core_n, 1)
        own_w = lax.dynamic_slice(out_weight, (0, kv_group * col_width), (rows_total, col_width))
        earlier = shift(paired, SEQ, cycle_size, 1)
        farther = shift(paired, SEQ, cycle_size, 2)
        context = jnp.concatenate([farther, earlier, paired], axis=1)
        context_blocks = context.shape[1]
        context_k = context[0].reshape(context_blocks * BLOCK_TOKENS, head_dim)
        context_v = context[1].reshape(context_blocks * BLOCK_TOKENS, head_dim)
        first_block = cycle_index * block_count
        query_block = first_block + jnp.arange(block_count, dtype=jnp.int32)
        key_block = (
            first_block
            - (context_blocks - block_count)
            + jnp.arange(context_blocks, dtype=jnp.int32)
        )
        distance_blk = query_block[:, None] - key_block[None, :]
        token_pos = jnp.arange(BLOCK_TOKENS)
        causal_tri = token_pos[None, :] <= token_pos[:, None]
        causal_ctx = jnp.tile(causal_tri, (block_count, context_blocks))
        query_heads = queries.reshape(token_count, local_heads, head_dim).transpose(1, 0, 2)
        score_diag = (
            jnp.einsum("htd,ud->htu", query_heads, context_k, preferred_element_type=jnp.float32)
            * score_scale
        )
        in_slash = jnp.any(distance_blk[None, None] == slash_group[:, :, None, None], axis=1)
        in_vert = jnp.any(key_block[None, None, :] == vert_group[:, :, None], axis=1)
        keep_blk = in_slash & (key_block >= 0)[None, None, :] & jnp.logical_not(in_vert)[:, None, :]
        whole_blk = keep_blk & (distance_blk != 0)[None]
        allow_diag = (
            spread(whole_blk, BLOCK_TOKENS, BLOCK_TOKENS)
            | spread(keep_blk & (distance_blk == 0)[None], BLOCK_TOKENS, BLOCK_TOKENS)
            & causal_ctx[None]
        )
        top_diag = jnp.max(jnp.where(allow_diag, score_diag, -jnp.inf), axis=2, keepdims=True)
        expo_diag = jnp.where(allow_diag, jnp.exp(score_diag - top_diag), 0.0)
        total_diag = jnp.sum(expo_diag, axis=2, keepdims=True)
        acc_diag = jnp.einsum(
            "htu,ud->htd",
            expo_diag.astype(jnp.bfloat16),
            context_v,
            preferred_element_type=jnp.float32,
        )
        arrived = arrived.reshape(2, cycle_size * capacity, BLOCK_TOKENS, head_dim)
        chosen = arrived[:, owner_dev * capacity + slot_index]
        vert_count = vert_group.shape[1]
        chosen = chosen.reshape(2, local_heads, vert_count * BLOCK_TOKENS, head_dim)
        score_vert = (
            jnp.einsum("htd,hud->htu", query_heads, chosen[0], preferred_element_type=jnp.float32)
            * score_scale
        )
        vert_cols = jnp.repeat(vert_group, BLOCK_TOKENS, axis=1)
        row_block = jnp.repeat(query_block, BLOCK_TOKENS)
        causal_vert = jnp.tile(causal_tri, (block_count, vert_count))
        allow_vert = (vert_cols[:, None, :] < row_block[None, :, None]) | (
            vert_cols[:, None, :] == row_block[None, :, None]
        ) & causal_vert[None]
        top_vert = jnp.max(jnp.where(allow_vert, score_vert, -jnp.inf), axis=2, keepdims=True)
        row_top = jnp.maximum(top_diag, top_vert)
        expo_vert = jnp.where(allow_vert, jnp.exp(score_vert - row_top), 0.0)
        diag_scale = jnp.exp(top_diag - row_top)
        row_total = total_diag * diag_scale + jnp.sum(expo_vert, axis=2, keepdims=True)
        acc_vert = jnp.einsum(
            "htu,hud->htd",
            expo_vert.astype(jnp.bfloat16),
            chosen[1],
            preferred_element_type=jnp.float32,
        )
        head_out = (acc_diag * diag_scale + acc_vert) / row_total
        attention = head_out.astype(jnp.bfloat16).transpose(1, 0, 2).reshape(token_count, -1)
        total = jnp.dot(attention, own_w, preferred_element_type=jnp.float32)
        for distance in range(1, heads_n):
            other = ring(attention, "heads", heads_n, distance)
            mine = lax.dynamic_slice_in_dim(other, core * half_rows, half_rows, 1)
            theirs = lax.dynamic_slice_in_dim(other, (1 - core) * half_rows, half_rows, 1)
            total = total + jnp.dot(mine, fetched[distance - 1], preferred_element_type=jnp.float32)
            total = total + jnp.dot(
                theirs, sibling_w[distance - 1], preferred_element_type=jnp.float32
            )
        return total.astype(jnp.bfloat16)

    return local


def split_mesh(mesh):
    devices = mesh.devices
    heads_n, seq_n = devices.shape
    core_n = 2
    y_n = len({d.coords[1] for d in devices.flat})
    z_n = seq_n // (core_n * y_n)
    sizes = (heads_n, z_n, y_n, core_n)
    return (Mesh(np.asarray(devices).reshape(sizes), ("heads",) + SEQ), sizes)


def solution(mesh):
    sub, sizes = split_mesh(mesh)
    return jax.shard_map(
        make_local(sizes),
        mesh=sub,
        in_specs=(P(SEQ, "heads"), P(SEQ, "heads"), P(SEQ, "heads"), P(), P(), P("heads", None)),
        out_specs=P(SEQ, "heads"),
        check_vma=False,
    )
```

profile of v0, /device:TPU:1, one launch (start us, length us, event | category | flops | bytes accessed | tf_op | source)
XLA Modules:
  0.0 151.8 jit_solution(9992068218329997265)
XLA Ops:
  6.5 0.8 constant_dynamic-slice_fusion
  7.3 0.1 reshape.360
  7.4 0.2 convert_reduce_fusion
  7.6 0.1 fusion.51
  7.7 1.7 %pad_maximum_fusion.1 = bf16[2,8,64,128]{3,2,1,0:T(8,128)(2,1)} fusion(bf16[1,8,64,128]{3,2,1,0:T(8,128)(2,1)} %bitcast.175, bf16[1,8,64,128]{3,2,1,0:T(8,128)(2,1)} %bitcast.177), kind=kLoop, calls=%fused_computation.41 | loop fusion | flops 131072 | bytes 524288 | tf_op jit(solution)/shard_map/stack | solution.py:46
  9.4 1.5 gather_fusion
  11.0 0.6 copy.27
  11.6 0.0 all-gather.2.cloned.1.call-update
  11.6 4.6 %collective-permute-start.1 = (bf16[2,8,64,128]{3,2,1,0:T(8,128)(2,1)}, bf16[2,8,64,128]{3,2,1,0:T(8,128)(2,1)}, u32[]{:S(2)}, u32[]{:S(2)}) collective-permute-start(bf16[2,8,64,128]{3,2,1,0:T(8,128)(2,1)} %pad_maximum_fusion.1), channel_id=1, source_target_pairs={{0,1},{1,2},{2,3},{3,4},{4,5},{5,6},{6,7},{7,8},{8,9},{9,10},{10,1... | collective-permute-start | bytes 786440 | tf_op jit(solution)/shard_map/ppermute | solution.py:16
  16.2 3.9 %collective-permute-start = (bf16[2,8,64,128]{3,2,1,0:T(8,128)(2,1)}, bf16[2,8,64,128]{3,2,1,0:T(8,128)(2,1)}, u32[]{:S(2)}, u32[]{:S(2)}) collective-permute-start(bf16[2,8,64,128]{3,2,1,0:T(8,128)(2,1)} %pad_maximum_fusion.1), channel_id=1, source_target_pairs={{0,2},{1,3},{2,4},{3,5},{4,6},{5,7},{6,8},{7,9},{8,10},{9,11},{10,... | collective-permute-start | bytes 786440 | tf_op jit(solution)/shard_map/ppermute | solution.py:16
  20.1 2.5 %fusion.57 = (bf16[256,1024]{1,0:T(8,128)(2,1)}, bf16[256,1024]{1,0:T(8,128)(2,1)}, bf16[256,1024]{1,0:T(8,128)(2,1)}) fusion(bf16[512,4096]{1,0:T(8,128)(2,1)} %param.11, s32[]{:T(128)S(6)} %select_n.128, s32[]{:T(128)S(6)} %select_n.130, s32[]{:T(128)S(6)} %select_n.135, s32[]{:T(128)S(6)} %select_n.133), kind=kLoop, calls=%fused_computation.100 | loop fusion | bytes 3145744 | tf_op jit(solution)/shard_map/dynamic_slice | solution.py:64
  22.6 2.5 %collective-permute-start.5 = (bf16[256,1024]{1,0:T(8,128)(2,1)}, bf16[256,1024]{1,0:T(8,128)(2,1)}, u32[]{:S(2)}, u32[]{:S(2)}) collective-permute-start(bf16[256,1024]{1,0:T(8,128)(2,1)} %get-tuple-element.12), channel_id=1, source_target_pairs={{0,192},{64,0},{128,64},{192,128},{1,193},{65,1},{129,65},{193,129... | collective-permute-start | bytes 1572872 | tf_op jit(solution)/shard_map/ppermute | solution.py:20
  25.1 0.5 collective-permute-start.4
  25.6 0.6 collective-permute-start.3
  26.2 0.1 reshape.363
  26.3 0.1 constant_dynamic-slice_fusion.1
  26.4 0.1 copy.21
  26.5 0.1 compare_reduce_fusion.1
  26.6 0.1 broadcast_subtract_fusion
  26.7 0.1 compare_reduce_fusion
  26.8 0.1 subtract_compare_fusion.1
  26.9 0.7 tile.4
  27.6 2.1 %and.141 = pred[512,1536]{0,1:T(8,128)(4,1)S(1)} reshape(pred[8,64,24,64]{1,0,3,2:T(8,128)(4,1)S(1)} %tile.4) | data formatting | bytes 1572864 | tf_op jit(solution)/shard_map/and | solution.py:99
  29.7 0.1 copy.23
  29.8 0.2 broadcast_in_dim.39
  30.0 0.2 reshape.357
  30.2 0.1 copy.22
  30.3 0.2 broadcast_in_dim.37
  30.5 0.2 reshape.355
  30.6 0.4 tile.5
  31.1 1.4 and.144
  32.5 0.1 broadcast_in_dim.77
  32.5 0.7 lt.99
  33.2 0.1 broadcast_in_dim.76
  33.3 0.7 lt.97
  34.0 0.6 pad_clamp_fusion
  34.6 1.1 maximum_maximum_fusion
  35.7 0.1 fusion.59
  35.8 3.4 %fusion = (f32[4,512]{1,0:T(4,128)S(1)}, f32[1536,4,512]{2,0,1:T(8,128)S(1)}) fusion(pred[512,1536]{0,1:T(8,128)(4,1)S(1)} %and.141, pred[4,512,24]{1,2,0:T(8,128)(4,1)S(1)} %reshape.357, pred[4,512,24]{1,2,0:T(8,128)(4,1)S(1)} %reshape.355, bf16[1536,128,1]{1,0,2:T(8,128)(2,1)S(1)} %bitcast.167, bf16[512,512]{1,0:T(8,128)(2,1)S(1)} %copy-done), kind=kOutput, calls=%fused_computation.4 | convolution fusion | flops 821032960 | bytes 14393344 | tf_op jit(solution)/shard_map/htd,ud->htu/dot_general | solution.py:90
  39.2 5.7 %fusion.7 = (f32[4,512]{1,0:T(4,128)S(1)}, bf16[4,512,1536]{1,2,0:T(8,128)(2,1)}) fusion(f32[1536,4,512]{2,0,1:T(8,128)S(1)} %get-tuple-element.23, f32[4,512]{1,0:T(4,128)S(1)} %get-tuple-element.22, pred[512,1536]{0,1:T(8,128)(4,1)S(1)} %and.141, pred[4,512,24]{1,2,0:T(8,128)(4,1)S(1)} %reshape.357, pred[4,512,24]{1,2,0:T(8,128)(4,1)S(1)} %reshape.355), kind=kLoop, calls=%fused_computation.15 | loop fusion | flops 22018048 | bytes 19775488 | tf_op jit(solution)/shard_map/reduce_sum | solution.py:104
  44.8 3.2 %collective-permute-done.5 = bf16[256,1024]{1,0:T(8,128)(2,1)} collective-permute-done((bf16[256,1024]{1,0:T(8,128)(2,1)}, bf16[256,1024]{1,0:T(8,128)(2,1)}, u32[]{:S(2)}, u32[]{:S(2)}) %collective-permute-start.5) | collective-permute-done | bytes 524320 | tf_op jit(solution)/shard_map/ppermute | solution.py:20
  48.0 3.9 %collective-permute-done.3 = bf16[256,1024]{1,0:T(8,128)(2,1)} collective-permute-done((bf16[256,1024]{1,0:T(8,128)(2,1)}, bf16[256,1024]{1,0:T(8,128)(2,1)}, u32[]{:S(2)}, u32[]{:S(2)}) %collective-permute-start.3) | collective-permute-done | bytes 524320 | tf_op jit(solution)/shard_map/ppermute | solution.py:20
  51.9 2.7 %pad_maximum_fusion = bf16[3,256,1024]{2,1,0:T(8,128)(2,1)} fusion(bf16[1,256,1024]{2,1,0:T(8,128)(2,1)} %bitcast.30, bf16[1,256,1024]{2,1,0:T(8,128)(2,1)} %bitcast.29, bf16[1,256,1024]{2,1,0:T(8,128)(2,1)} %bitcast.28), kind=kLoop, calls=%fused_computation.21 | loop fusion | flops 1572864 | bytes 3145728 | tf_op jit(solution)/shard_map/stack | solution.py:68
  54.7 0.4 collective-permute-start.6
  55.1 40.0 %all-gather.2.cloned.1.call-done = bf16[2,8192,128]{2,1,0:T(8,128)(2,1)} async-done(((bf16[2,128,128]{2,1,0:T(8,128)(2,1)}), bf16[2,8192,128]{2,1,0:T(8,128)(2,1)}) %all-gather.2.cloned.1.call-update) | async-done | bytes 4194320 | tf_op jit(solution)/shard_map/all_gather | solution.py:57
  95.1 3.3 %gather_fusion.1 = bf16[64,2,64,128]{3,2,1,0:T(8,128)(2,1)S(1)} fusion(bf16[2,128,64,128]{3,2,1,0:T(8,128)(2,1)} %bitcast.172, s32[1024]{0:T(1024)} %pad_clamp_fusion), kind=kCustom, calls=%fused_computation.1 | custom fusion | bytes 4194560 | tf_op jit(solution)/shard_map/gather | solution.py:112
  98.4 0.2 fusion.58
  98.6 0.5 copy-done.4
  99.1 3.0 %fusion.4 = (f32[4,512]{1,0:T(4,128)S(1)}, f32[4,1024,512]{2,1,0:T(8,128)S(1)}) fusion(pred[512,1024]{0,1:T(8,128)(4,1)S(1)} %and.144, s32[512]{0:T(512)S(1)} %copy-done.5, s32[4,1024]{1,0:T(4,128)S(1)} %copy-done.4, bf16[4,1024,128]{2,1,0:T(8,128)(2,1)S(1)} %bitcast.174, bf16[512,512]{1,0:T(8,128)(2,1)S(1)} %copy-done), kind=kOutput, calls=%fused_computation.11 | convolution fusion | flops 551548928 | bytes 10512384 | tf_op jit(solution)/shard_map/htd,hud->htu/dot_general | solution.py:116
  102.1 3.8 %fusion.9 = f32[4,512]{1,0:T(4,128)S(1)} fusion(f32[4,1024,512]{2,1,0:T(8,128)S(1)} %get-tuple-element.25, f32[4,512]{1,0:T(4,128)S(1)} %max.19, pred[512,1024]{0,1:T(8,128)(4,1)S(1)} %and.144, s32[512]{0:T(512)S(1)} %copy-done.5, s32[4,1024]{1,0:T(4,128)S(1)} %copy-done.4), kind=kLoop, calls=%fused_computation.17 | loop fusion | flops 16775168 | bytes 8947712 | tf_op jit(solution)/shard_map/reduce_sum | solution.py:129
  106.0 1.1 fusion.16
  107.1 3.8 %divide_convert_fusion = bf16[512,4,128]{0,2,1:T(8,128)(2,1)S(1)} fusion(f32[512,4,128]{0,2,1:T(8,128)S(1)} %fusion.16, bf16[4,1024,128]{2,1,0:T(8,128)(2,1)S(1)} %bitcast.173, f32[4,1024,512]{2,1,0:T(8,128)S(1)} %get-tuple-element.25, f32[4,512]{1,0:T(4,128)S(1)} %max.19, f32[512,4]{0,1:T(4,128)S(1)} %get-tuple-element.5, s32[512]{0:T(512)S(1)} %copy-done.5, ...), kind=kOutput, calls=%fused_computation.28 | convolution fusion | flops 554434560 | bytes 11569152 | tf_op jit(solution)/shard_map/htu,hud->htd/dot_general | solution.py:130
  110.9 2.8 %collective-permute-start.7 = (bf16[512,512]{0,1:T(8,128)(2,1)S(1)}, bf16[512,512]{0,1:T(8,128)(2,1)S(1)}, u32[]{:S(2)}, u32[]{:S(2)}) collective-permute-start(bf16[512,512]{0,1:T(8,128)(2,1)S(1)} %bitcast.168), channel_id=1, source_target_pairs={{0,128},{64,192},{128,0},{192,64},{1,129},{65,193},{129,1},{193,65... | collective-permute-start | bytes 1572872 | tf_op jit(solution)/shard_map/ppermute | solution.py:20
  113.7 0.9 collective-permute-start.8
  114.6 0.6 collective-permute-start.2
  115.2 1.9 %fusion.20 = f32[512,1024]{1,0:T(8,128)S(1)} fusion(bf16[512,512]{0,1:T(8,128)(2,1)S(1)} %bitcast.171, bf16[512,4096]{1,0:T(8,128)(2,1)} %param.11, s32[]{:T(128)S(6)} %select_n.127), kind=kOutput, calls=%fused_computation.26 | convolution fusion | flops 536870912 | bytes 3670020 | tf_op jit(solution)/shard_map/dot_general | solution.py:138
  117.1 8.6 %collective-permute-done.7 = bf16[512,512]{0,1:T(8,128)(2,1)S(1)} collective-permute-done((bf16[512,512]{0,1:T(8,128)(2,1)S(1)}, bf16[512,512]{0,1:T(8,128)(2,1)S(1)}, u32[]{:S(2)}, u32[]{:S(2)}) %collective-permute-start.7) | collective-permute-done | bytes 524320 | tf_op jit(solution)/shard_map/ppermute | solution.py:20
  125.7 1.5 fusion.35
  127.2 1.5 fusion.27
  128.8 8.8 %collective-permute-done.2 = bf16[512,512]{0,1:T(8,128)(2,1)S(1)} collective-permute-done((bf16[512,512]{0,1:T(8,128)(2,1)S(1)}, bf16[512,512]{0,1:T(8,128)(2,1)S(1)}, u32[]{:S(2)}, u32[]{:S(2)}) %collective-permute-start.2) | collective-permute-done | bytes 524320 | tf_op jit(solution)/shard_map/ppermute | solution.py:20
  137.6 1.5 fusion.28
  139.1 1.5 fusion.38
  140.6 1.5 fusion.32
  142.1 2.8 %add_convert_fusion = bf16[512,1024]{1,0:T(8,128)(2,1)} fusion(f32[512,1024]{1,0:T(8,128)S(1)} %fusion.32, f32[512,1024]{1,0:T(8,128)S(1)} %fusion.27, f32[512,1024]{1,0:T(8,128)S(1)} %fusion.35, f32[512,1024]{1,0:T(8,128)S(1)} %fusion.28, f32[512,1024]{1,0:T(8,128)S(1)} %fusion.20, f32[512,1024]{1,0:T(8,128)S(1)} %fusion.38, ...), kind=kOutput, calls=%fused_computation.20 | convolution fusion | flops 272105472 | bytes 14417924 | tf_op jit(solution)/shard_map/dot_general | solution.py:144
  (37 shorter events, 0.2 us)
Async XLA Ops:
  6.5 29.2 %copy-start = (bf16[512,512]{1,0:T(8,128)(2,1)S(1)}, bf16[512,512]{1,0:T(8,128)(2,1)}, u32[]{:S(2)}) copy-start(bf16[512,512]{1,0:T(8,128)(2,1)} %param.6) | copy-start | bytes 1572868
  6.5 19.8 %copy-start.6 = (s32[16,8]{0,1:T(8,128)S(1)}, s32[16,8]{0,1:T(8,128)}, u32[]{:S(2)}) copy-start(s32[16,8]{0,1:T(8,128)} %param.10) | copy-start | bytes 1540
  6.5 88.5 %all-gather.2.cloned.1.call-start = ((), (), s32[]{:S(2)}) async-start(), calls=%async_computation | async-start | bytes 4259840 | tf_op jit(solution)/shard_map/all_gather | solution.py:57
  11.6 23.0 %collective-permute-start.1 = (bf16[2,8,64,128]{3,2,1,0:T(8,128)(2,1)}, bf16[2,8,64,128]{3,2,1,0:T(8,128)(2,1)}, u32[]{:S(2)}, u32[]{:S(2)}) collective-permute-start(bf16[2,8,64,128]{3,2,1,0:T(8,128)(2,1)} %pad_maximum_fusion.1), channel_id=1, source_target_pairs={{0,1},{1,2},{2,3},{3,4},{4,5},{5,6},{6,7},{7,8},{8,9},{9,10},{10,1... | collective-permute-start | bytes 786440 | tf_op jit(solution)/shard_map/ppermute | solution.py:16
  16.2 18.4 %collective-permute-start = (bf16[2,8,64,128]{3,2,1,0:T(8,128)(2,1)}, bf16[2,8,64,128]{3,2,1,0:T(8,128)(2,1)}, u32[]{:S(2)}, u32[]{:S(2)}) collective-permute-start(bf16[2,8,64,128]{3,2,1,0:T(8,128)(2,1)} %pad_maximum_fusion.1), channel_id=1, source_target_pairs={{0,2},{1,3},{2,4},{3,5},{4,6},{5,7},{6,8},{7,9},{8,10},{9,11},{10,... | collective-permute-start | bytes 786440 | tf_op jit(solution)/shard_map/ppermute | solution.py:16
  22.6 25.4 %collective-permute-start.5 = (bf16[256,1024]{1,0:T(8,128)(2,1)}, bf16[256,1024]{1,0:T(8,128)(2,1)}, u32[]{:S(2)}, u32[]{:S(2)}) collective-permute-start(bf16[256,1024]{1,0:T(8,128)(2,1)} %get-tuple-element.12), channel_id=1, source_target_pairs={{0,192},{64,0},{128,64},{192,128},{1,193},{65,1},{129,65},{193,129... | collective-permute-start | bytes 1572872 | tf_op jit(solution)/shard_map/ppermute | solution.py:20
  25.1 22.9 %collective-permute-start.4 = (bf16[256,1024]{1,0:T(8,128)(2,1)}, bf16[256,1024]{1,0:T(8,128)(2,1)}, u32[]{:S(2)}, u32[]{:S(2)}) collective-permute-start(bf16[256,1024]{1,0:T(8,128)(2,1)} %get-tuple-element.13), channel_id=1, source_target_pairs={{0,128},{64,192},{128,0},{192,64},{1,129},{65,193},{129,1},{193,65... | collective-permute-start | bytes 1572872 | tf_op jit(solution)/shard_map/ppermute | solution.py:20
  25.6 26.3 %collective-permute-start.3 = (bf16[256,1024]{1,0:T(8,128)(2,1)}, bf16[256,1024]{1,0:T(8,128)(2,1)}, u32[]{:S(2)}, u32[]{:S(2)}) collective-permute-start(bf16[256,1024]{1,0:T(8,128)(2,1)} %get-tuple-element.11), channel_id=1, source_target_pairs={{0,64},{64,128},{128,192},{192,0},{1,65},{65,129},{129,193},{193,1... | collective-permute-start | bytes 1572872 | tf_op jit(solution)/shard_map/ppermute | solution.py:20
  27.6 7.0 %copy-start.2 = (bf16[512,128]{1,0:T(8,128)(2,1)S(1)}, bf16[512,128]{1,0:T(8,128)(2,1)}, u32[]{:S(2)}) copy-start(bf16[512,128]{1,0:T(8,128)(2,1)} %param.8) | copy-start | bytes 393220
  29.7 4.9 %copy-start.3 = (bf16[512,128]{1,0:T(8,128)(2,1)S(1)}, bf16[512,128]{1,0:T(8,128)(2,1)}, u32[]{:S(2)}) copy-start(bf16[512,128]{1,0:T(8,128)(2,1)} %param.7) | copy-start | bytes 393220
  54.7 72.6 %collective-permute-start.6 = (bf16[3,256,1024]{2,1,0:T(8,128)(2,1)}, bf16[3,256,1024]{2,1,0:T(8,128)(2,1)}, u32[]{:S(2)}, u32[]{:S(2)}) collective-permute-start(bf16[3,256,1024]{2,1,0:T(8,128)(2,1)} %pad_maximum_fusion), channel_id=1, source_target_pairs={{0,1},{1,0},{2,3},{3,2},{4,5},{5,4},{6,7},{7,6},{8,9},{9,8},{10,11... | collective-permute-start | bytes 4718600 | tf_op jit(solution)/shard_map/ppermute | solution.py:20
  98.3 0.7 copy-start.4
  98.3 0.7 copy-start.5
  98.4 7.6 %slice-start = ((s8[6291456]{0:T(1024)(128)(4,1)}), s8[4194304]{0:T(1024)(128)(4,1)S(1)}, s32[]{:S(2)}) async-start(s8[6291456]{0:T(1024)(128)(4,1)} %bitcast.165), calls=%async_computation.1 | async-start | bytes 8388608
  99.1 6.9 %slice-start.1 = ((s8[6291456]{0:T(1024)(128)(4,1)}), s8[2097152]{0:T(1024)(128)(4,1)S(1)}, s32[]{:S(2)}) async-start(s8[6291456]{0:T(1024)(128)(4,1)} %bitcast.165), calls=%async_computation.2 | async-start | bytes 4194304
  110.9 14.8 %collective-permute-start.7 = (bf16[512,512]{0,1:T(8,128)(2,1)S(1)}, bf16[512,512]{0,1:T(8,128)(2,1)S(1)}, u32[]{:S(2)}, u32[]{:S(2)}) collective-permute-start(bf16[512,512]{0,1:T(8,128)(2,1)S(1)} %bitcast.168), channel_id=1, source_target_pairs={{0,128},{64,192},{128,0},{192,64},{1,129},{65,193},{129,1},{193,65... | collective-permute-start | bytes 1572872 | tf_op jit(solution)/shard_map/ppermute | solution.py:20
  113.7 26.9 %collective-permute-start.8 = (bf16[512,512]{0,1:T(8,128)(2,1)S(1)}, bf16[512,512]{0,1:T(8,128)(2,1)S(1)}, u32[]{:S(2)}, u32[]{:S(2)}) collective-permute-start(bf16[512,512]{0,1:T(8,128)(2,1)S(1)} %bitcast.169), channel_id=1, source_target_pairs={{0,192},{64,0},{128,64},{192,128},{1,193},{65,1},{129,65},{193,129... | collective-permute-start | bytes 1572872 | tf_op jit(solution)/shard_map/ppermute | solution.py:20
  114.6 23.0 %collective-permute-start.2 = (bf16[512,512]{0,1:T(8,128)(2,1)S(1)}, bf16[512,512]{0,1:T(8,128)(2,1)S(1)}, u32[]{:S(2)}, u32[]{:S(2)}) collective-permute-start(bf16[512,512]{0,1:T(8,128)(2,1)S(1)} %bitcast.170), channel_id=1, source_target_pairs={{0,64},{64,128},{128,192},{192,0},{1,65},{65,129},{129,193},{193,1... | collective-permute-start | bytes 1572872 | tf_op jit(solution)/shard_map/ppermute | solution.py:20
  142.1 2.8 %copy-start.1 = (bf16[512,512]{1,0:T(8,128)(2,1)S(1)}, bf16[512,512]{1,0:T(8,128)(2,1)}, u32[]{:S(2)}) copy-start(bf16[512,512]{1,0:T(8,128)(2,1)} %param.6) | copy-start | bytes 1572868
Sparse Core Ops, SparseCore 0:
  11.7 83.3 all-gather.1
where the time goes:
time: 152 us
  waiting for transfers between devices  64.6 us (42%)
  matrix products  23.6 us (16%)
  local copies, waits for them, and re-layouts  16.7 us (11%)
  starting transfers between devices  16.7 us (11%)
  other arithmetic  16.4 us (11%)
  between operations  13.7 us (9%)
    all_gather x1, waiting for transfers between devices, local(): arrived = lax.all_gather(outgoing, SEQ, axis=1, tiled=True)  40 us
    ppermute x7, waiting for transfers between devices, ring(): lax.ppermute(block, axis, [(i, (i + distance) % size) for i in range(size)])  24.6 us
    ppermute x2, starting transfers between devices, shift(): return lax.ppermute(block, axis, route)  8.48 us
    ppermute x7, starting transfers between devices, ring(): lax.ppermute(block, axis, [(i, (i + distance) % size) for i in range(size)])  8.26 us
    dot_general x3, matrix products, local(): jnp.dot(theirs, sibling_w[distance - 1], preferred_element_type=jnp.float32)  5.82 us
    reduce_sum x1, other arithmetic, local(): total_diag = jnp.sum(expo_diag, axis=2, keepdims=True)  5.65 us
    dot_general x3, matrix products, local(): jnp.dot(mine, fetched[distance - 1], preferred_element_type=jnp.float32)  4.51 us
    reduce_sum x1, other arithmetic, local(): jnp.sum(expo_vert, axis=2, keepdims=True)  3.83 us
  transfers between devices with their start and end apart: 10, of which 5 were waited for; matrix products, arithmetic and copies ran while one was open for 31% of the time, Pallas kernels for 0%

commit v1 on v0

--- a/solution.py
+++ b/solution.py
@@ -54,7 +54,9 @@
         selector = owned_here[None, :] & (slot_index[None, :] == jnp.arange(capacity)[:, None])
         picked = jnp.sum(jnp.where(selector, within_dev[None, :], 0), axis=1)
         outgoing = paired[:, picked].reshape(2, capacity * BLOCK_TOKENS, head_dim)
-        arrived = lax.all_gather(outgoing, SEQ, axis=1, tiled=True)
+        arrived = jnp.concatenate(
+            lax.all_to_all(jnp.stack([outgoing] * lax.axis_size(SEQ)), SEQ, 0, 0), axis=1
+        )
         rows_total, width = out_weight.shape
         col_width = width // heads_n
         half_rows = rows_total // core_n

time: 152 us -> 190 us (1.25)
  the two profiles are of different devices: /device:TPU:1 before, /device:TPU:37 now
where the time goes in v1:
time: 190 us; the launch traced here: 189 us
  waiting for transfers between devices  101 us (53%)
  local copies, waits for them, and re-layouts  24.1 us (13%)
  starting transfers between devices  23.6 us (12%)
  matrix products  23.6 us (12%)
  other arithmetic  16.3 us (9%)
    ppermute x2, waiting for transfers between devices, shift(): return lax.ppermute(block, axis, route)  81.3 us
    ppermute x7, waiting for transfers between devices, ring(): lax.ppermute(block, axis, [(i, (i + distance) % size) for i in range(size)])  19.5 us
    all_to_all x1, starting transfers between devices, local(): lax.all_to_all(jnp.stack([outgoing] * lax.axis_size(SEQ)), SEQ, 0, 0)  12.2 us
    ppermute x2, starting transfers between devices, shift(): return lax.ppermute(block, axis, route)  6.47 us
    dot_general x3, matrix products, local(): jnp.dot(theirs, sibling_w[distance - 1], preferred_element_type=jnp.float32)  5.82 us
    reduce_sum x1, other arithmetic, local(): total_diag = jnp.sum(expo_diag, axis=2, keepdims=True)  5.64 us
    ppermute x7, starting transfers between devices, ring(): lax.ppermute(block, axis, [(i, (i + distance) % size) for i in range(size)])  4.9 us
    all_to_all x1, local copies, waits for them, and re-layouts, local(): lax.all_to_all(jnp.stack([outgoing] * lax.axis_size(SEQ)), SEQ, 0, 0)  4.83 us
  transfers between devices with their start and end apart: 10, of which 3 were waited for; matrix products, arithmetic and copies ran while one was open for 27% of the time, Pallas kernels for 0%

profile of v1, /device:TPU:37, one launch (start us, length us, event | category | flops | bytes accessed | tf_op | source)
XLA Modules:
  0.0 188.8 jit_solution(4227775659782177344)
XLA Ops:
  0.0 0.7 constant_dynamic-slice_fusion
  0.8 0.1 reshape.359
  0.9 0.2 convert_reduce_fusion
  1.0 0.1 fusion.51
  1.2 1.7 pad_maximum_fusion.1
  2.9 1.5 gather_fusion
  4.4 3.1 %stack.27 = bf16[64,2,128,128]{3,2,1,0:T(8,128)(2,1)} broadcast(bf16[2,128,128]{2,1,0:T(8,128)(2,1)S(1)} %bitcast.182), dimensions={1,2,3} | broadcast | bytes 4259840 | tf_op jit(solution)/shard_map/stack | solution.py:58
  7.5 12.2 %all-to-all-start = ((bf16[64,2,128,128]{3,2,1,0:T(8,128)(2,1)}), bf16[64,2,128,128]{3,2,1,0:T(8,128)(2,1)}, u32[]{:S(2)}, u32[]{:S(2)}) async-start(bf16[64,2,128,128]{3,2,1,0:T(8,128)(2,1)} %stack.27), calls=%async_computation | async-start | bytes 8388608 | tf_op jit(solution)/shard_map/all_to_all | solution.py:58
  19.8 0.0 copy-start.6
  19.8 3.4 %collective-permute-start.1 = (bf16[2,8,64,128]{3,2,1,0:T(8,128)(2,1)}, bf16[2,8,64,128]{3,2,1,0:T(8,128)(2,1)}, u32[]{:S(2)}, u32[]{:S(2)}) collective-permute-start(bf16[2,8,64,128]{3,2,1,0:T(8,128)(2,1)} %pad_maximum_fusion.1), channel_id=1, source_target_pairs={{0,1},{1,2},{2,3},{3,4},{4,5},{5,6},{6,7},{7,8},{8,9},{9,10},{10,1... | collective-permute-start | bytes 786440 | tf_op jit(solution)/shard_map/ppermute | solution.py:16
  23.2 3.1 %collective-permute-start = (bf16[2,8,64,128]{3,2,1,0:T(8,128)(2,1)}, bf16[2,8,64,128]{3,2,1,0:T(8,128)(2,1)}, u32[]{:S(2)}, u32[]{:S(2)}) collective-permute-start(bf16[2,8,64,128]{3,2,1,0:T(8,128)(2,1)} %pad_maximum_fusion.1), channel_id=1, source_target_pairs={{0,2},{1,3},{2,4},{3,5},{4,6},{5,7},{6,8},{7,9},{8,10},{9,11},{10,... | collective-permute-start | bytes 786440 | tf_op jit(solution)/shard_map/ppermute | solution.py:16
  26.3 2.6 %fusion.57 = (bf16[256,1024]{1,0:T(8,128)(2,1)}, bf16[256,1024]{1,0:T(8,128)(2,1)}, bf16[256,1024]{1,0:T(8,128)(2,1)}) fusion(bf16[512,4096]{1,0:T(8,128)(2,1)} %param.11, s32[]{:T(128)S(6)} %select_n.128, s32[]{:T(128)S(6)} %select_n.130, s32[]{:T(128)S(6)} %select_n.135, s32[]{:T(128)S(6)} %select_n.133), kind=kLoop, calls=%fused_computation.100 | loop fusion | bytes 3145744 | tf_op jit(solution)/shard_map/dynamic_slice | solution.py:66
  28.9 0.3 collective-permute-start.5
  29.1 2.5 %collective-permute-start.4 = (bf16[256,1024]{1,0:T(8,128)(2,1)}, bf16[256,1024]{1,0:T(8,128)(2,1)}, u32[]{:S(2)}, u32[]{:S(2)}) collective-permute-start(bf16[256,1024]{1,0:T(8,128)(2,1)} %get-tuple-element.13), channel_id=1, source_target_pairs={{0,128},{64,192},{128,0},{192,64},{1,129},{65,193},{129,1},{193,65... | collective-permute-start | bytes 1572872 | tf_op jit(solution)/shard_map/ppermute | solution.py:20
  31.6 0.1 reshape.361
  31.7 0.1 constant_dynamic-slice_fusion.1
  31.7 0.1 copy.30
  31.8 0.1 compare_reduce_fusion.1
  32.0 0.1 broadcast_subtract_fusion
  32.0 0.1 compare_reduce_fusion
  32.1 0.1 subtract_compare_fusion.1
  32.3 0.7 tile.4
  32.9 0.0 copy-start.2
  32.9 2.1 %and.141 = pred[512,1536]{0,1:T(8,128)(4,1)S(1)} reshape(pred[8,64,24,64]{1,0,3,2:T(8,128)(4,1)S(1)} %tile.4) | data formatting | bytes 1572864 | tf_op jit(solution)/shard_map/and | solution.py:101
  35.1 0.0 copy-start.3
  35.1 0.1 copy.32
  35.2 0.2 broadcast_in_dim.39
  35.3 0.2 reshape.356
  35.5 0.1 copy.31
  35.6 0.2 broadcast_in_dim.37
  35.8 0.2 reshape.354
  36.0 0.4 tile.5
  36.4 1.4 and.144
  37.8 0.1 broadcast_in_dim.77
  37.9 0.7 lt.99
  38.6 0.1 broadcast_in_dim.76
  38.6 0.7 lt.97
  39.3 0.6 pad_clamp_fusion
  39.9 81.3 %collective-permute-done = bf16[2,8,64,128]{3,2,1,0:T(8,128)(2,1)} collective-permute-done((bf16[2,8,64,128]{3,2,1,0:T(8,128)(2,1)}, bf16[2,8,64,128]{3,2,1,0:T(8,128)(2,1)}, u32[]{:S(2)}, u32[]{:S(2)}) %collective-permute-start) | collective-permute-done | bytes 262176 | tf_op jit(solution)/shard_map/ppermute | solution.py:16
  121.2 1.1 maximum_maximum_fusion
  122.3 0.1 fusion.59
  122.4 3.4 %fusion = (f32[4,512]{1,0:T(4,128)S(1)}, f32[1536,4,512]{2,0,1:T(8,128)S(1)}) fusion(pred[512,1536]{0,1:T(8,128)(4,1)S(1)} %and.141, pred[4,512,24]{1,2,0:T(8,128)(4,1)S(1)} %reshape.356, pred[4,512,24]{1,2,0:T(8,128)(4,1)S(1)} %reshape.354, bf16[1536,128,1]{1,0,2:T(8,128)(2,1)S(1)} %bitcast.170, bf16[512,512]{1,0:T(8,128)(2,1)S(1)} %copy-done), kind=kOutput, calls=%fused_computation.4 | convolution fusion | flops 821032960 | bytes 14393344 | tf_op jit(solution)/shard_map/htd,ud->htu/dot_general | solution.py:92
  125.8 5.6 %fusion.7 = (f32[4,512]{1,0:T(4,128)S(1)}, bf16[4,512,1536]{1,2,0:T(8,128)(2,1)}) fusion(f32[1536,4,512]{2,0,1:T(8,128)S(1)} %get-tuple-element.23, f32[4,512]{1,0:T(4,128)S(1)} %get-tuple-element.22, pred[512,1536]{0,1:T(8,128)(4,1)S(1)} %and.141, pred[4,512,24]{1,2,0:T(8,128)(4,1)S(1)} %reshape.356, pred[4,512,24]{1,2,0:T(8,128)(4,1)S(1)} %reshape.354), kind=kLoop, calls=%fused_computation.15 | loop fusion | flops 22018048 | bytes 19775488 | tf_op jit(solution)/shard_map/reduce_sum | solution.py:106
  131.4 2.7 %pad_maximum_fusion = bf16[3,256,1024]{2,1,0:T(8,128)(2,1)} fusion(bf16[1,256,1024]{2,1,0:T(8,128)(2,1)} %bitcast.31, bf16[1,256,1024]{2,1,0:T(8,128)(2,1)} %bitcast.30, bf16[1,256,1024]{2,1,0:T(8,128)(2,1)} %bitcast.29), kind=kLoop, calls=%fused_computation.21 | loop fusion | flops 1572864 | bytes 3145728 | tf_op jit(solution)/shard_map/stack | solution.py:70
  134.1 4.8 %copy.37 = bf16[64,2,128,128]{3,2,0,1:T(8,128)(2,1)} copy(bf16[64,2,128,128]{3,2,1,0:T(8,128)(2,1)} %all-to-all-done) | data formatting | bytes 8388608 | tf_op jit(solution)/shard_map/all_to_all | solution.py:58
  138.9 3.3 %gather_fusion.1 = bf16[64,2,64,128]{3,2,1,0:T(8,128)(2,1)S(1)} fusion(bf16[2,128,64,128]{3,2,1,0:T(8,128)(2,1)} %bitcast.166, s32[1024]{0:T(1024)} %pad_clamp_fusion), kind=kCustom, calls=%fused_computation.1 | custom fusion | bytes 4194560 | tf_op jit(solution)/shard_map/gather | solution.py:114
  142.2 0.2 fusion.58
  142.4 0.5 copy-done.4
  142.9 3.0 %fusion.4 = (f32[4,512]{1,0:T(4,128)S(1)}, f32[4,1024,512]{2,1,0:T(8,128)S(1)}) fusion(pred[512,1024]{0,1:T(8,128)(4,1)S(1)} %and.144, s32[512]{0:T(512)S(1)} %copy-done.5, s32[4,1024]{1,0:T(4,128)S(1)} %copy-done.4, bf16[4,1024,128]{2,1,0:T(8,128)(2,1)S(1)} %bitcast.176, bf16[512,512]{1,0:T(8,128)(2,1)S(1)} %copy-done), kind=kOutput, calls=%fused_computation.11 | convolution fusion | flops 551548928 | bytes 10512384 | tf_op jit(solution)/shard_map/htd,hud->htu/dot_general | solution.py:118
  146.0 3.8 %fusion.9 = f32[4,512]{1,0:T(4,128)S(1)} fusion(f32[4,1024,512]{2,1,0:T(8,128)S(1)} %get-tuple-element.25, f32[4,512]{1,0:T(4,128)S(1)} %max.19, pred[512,1024]{0,1:T(8,128)(4,1)S(1)} %and.144, s32[512]{0:T(512)S(1)} %copy-done.5, s32[4,1024]{1,0:T(4,128)S(1)} %copy-done.4), kind=kLoop, calls=%fused_computation.17 | loop fusion | flops 16775168 | bytes 8947712 | tf_op jit(solution)/shard_map/reduce_sum | solution.py:131
  149.9 1.1 fusion.16
  150.9 3.8 %divide_convert_fusion = bf16[512,4,128]{0,2,1:T(8,128)(2,1)S(1)} fusion(f32[512,4,128]{0,2,1:T(8,128)S(1)} %fusion.16, bf16[4,1024,128]{2,1,0:T(8,128)(2,1)S(1)} %bitcast.175, f32[4,1024,512]{2,1,0:T(8,128)S(1)} %get-tuple-element.25, f32[4,512]{1,0:T(4,128)S(1)} %max.19, f32[512,4]{0,1:T(4,128)S(1)} %get-tuple-element.5, s32[512]{0:T(512)S(1)} %copy-done.5, ...), kind=kOutput, calls=%fused_computation.28 | convolution fusion | flops 554434560 | bytes 11569152 | tf_op jit(solution)/shard_map/htu,hud->htd/dot_general | solution.py:132
  154.8 0.3 collective-permute-start.7
  155.1 1.9 collective-permute-start.8
  157.0 1.9 %fusion.20 = f32[512,1024]{1,0:T(8,128)S(1)} fusion(bf16[512,512]{0,1:T(8,128)(2,1)S(1)} %bitcast.174, bf16[512,4096]{1,0:T(8,128)(2,1)} %param.11, s32[]{:T(128)S(6)} %select_n.127), kind=kOutput, calls=%fused_computation.26 | convolution fusion | flops 536870912 | bytes 3670020 | tf_op jit(solution)/shard_map/dot_general | solution.py:140
  158.9 10.5 %collective-permute-done.7 = bf16[512,512]{0,1:T(8,128)(2,1)S(1)} collective-permute-done((bf16[512,512]{0,1:T(8,128)(2,1)S(1)}, bf16[512,512]{0,1:T(8,128)(2,1)S(1)}, u32[]{:S(2)}, u32[]{:S(2)}) %collective-permute-start.7) | collective-permute-done | bytes 524320 | tf_op jit(solution)/shard_map/ppermute | solution.py:20
  169.4 1.5 fusion.35
  170.9 1.5 fusion.27
  172.4 9.0 %collective-permute-done.2 = bf16[512,512]{0,1:T(8,128)(2,1)S(1)} collective-permute-done((bf16[512,512]{0,1:T(8,128)(2,1)S(1)}, bf16[512,512]{0,1:T(8,128)(2,1)S(1)}, u32[]{:S(2)}, u32[]{:S(2)}) %collective-permute-start.2) | collective-permute-done | bytes 524320 | tf_op jit(solution)/shard_map/ppermute | solution.py:20
  181.4 1.5 fusion.28
  182.9 1.5 fusion.38
  184.5 1.5 fusion.32
  186.0 0.0 copy-start.1
  186.0 2.8 %add_convert_fusion = bf16[512,1024]{1,0:T(8,128)(2,1)} fusion(f32[512,1024]{1,0:T(8,128)S(1)} %fusion.32, f32[512,1024]{1,0:T(8,128)S(1)} %fusion.27, f32[512,1024]{1,0:T(8,128)S(1)} %fusion.35, f32[512,1024]{1,0:T(8,128)S(1)} %fusion.28, f32[512,1024]{1,0:T(8,128)S(1)} %fusion.20, f32[512,1024]{1,0:T(8,128)S(1)} %fusion.38, ...), kind=kOutput, calls=%fused_computation.20 | convolution fusion | flops 272105472 | bytes 14417924 | tf_op jit(solution)/shard_map/dot_general | solution.py:146
  (38 shorter events, 0.2 us)
Async XLA Ops:
  0.0 122.4 %copy-start = (bf16[512,512]{1,0:T(8,128)(2,1)S(1)}, bf16[512,512]{1,0:T(8,128)(2,1)}, u32[]{:S(2)}) copy-start(bf16[512,512]{1,0:T(8,128)(2,1)} %param.6) | copy-start | bytes 1572868
  7.5 126.6 %all-to-all-start = ((bf16[64,2,128,128]{3,2,1,0:T(8,128)(2,1)}), bf16[64,2,128,128]{3,2,1,0:T(8,128)(2,1)}, u32[]{:S(2)}, u32[]{:S(2)}) async-start(bf16[64,2,128,128]{3,2,1,0:T(8,128)(2,1)} %stack.27), calls=%async_computation | async-start | bytes 8388608 | tf_op jit(solution)/shard_map/all_to_all | solution.py:58
  19.8 11.9 %copy-start.6 = (s32[16,8]{0,1:T(8,128)S(1)}, s32[16,8]{0,1:T(8,128)}, u32[]{:S(2)}) copy-start(s32[16,8]{0,1:T(8,128)} %param.10) | copy-start | bytes 1540
  19.8 20.1 %collective-permute-start.1 = (bf16[2,8,64,128]{3,2,1,0:T(8,128)(2,1)}, bf16[2,8,64,128]{3,2,1,0:T(8,128)(2,1)}, u32[]{:S(2)}, u32[]{:S(2)}) collective-permute-start(bf16[2,8,64,128]{3,2,1,0:T(8,128)(2,1)} %pad_maximum_fusion.1), channel_id=1, source_target_pairs={{0,1},{1,2},{2,3},{3,4},{4,5},{5,6},{6,7},{7,8},{8,9},{9,10},{10,1... | collective-permute-start | bytes 786440 | tf_op jit(solution)/shard_map/ppermute | solution.py:16
  23.2 98.0 %collective-permute-start = (bf16[2,8,64,128]{3,2,1,0:T(8,128)(2,1)}, bf16[2,8,64,128]{3,2,1,0:T(8,128)(2,1)}, u32[]{:S(2)}, u32[]{:S(2)}) collective-permute-start(bf16[2,8,64,128]{3,2,1,0:T(8,128)(2,1)} %pad_maximum_fusion.1), channel_id=1, source_target_pairs={{0,2},{1,3},{2,4},{3,5},{4,6},{5,7},{6,8},{7,9},{8,10},{9,11},{10,... | collective-permute-start | bytes 786440 | tf_op jit(solution)/shard_map/ppermute | solution.py:16
  28.9 102.5 %collective-permute-start.5 = (bf16[256,1024]{1,0:T(8,128)(2,1)}, bf16[256,1024]{1,0:T(8,128)(2,1)}, u32[]{:S(2)}, u32[]{:S(2)}) collective-permute-start(bf16[256,1024]{1,0:T(8,128)(2,1)} %get-tuple-element.12), channel_id=1, source_target_pairs={{0,192},{64,0},{128,64},{192,128},{1,193},{65,1},{129,65},{193,129... | collective-permute-start | bytes 1572872 | tf_op jit(solution)/shard_map/ppermute | solution.py:20
  29.1 102.3 %collective-permute-start.4 = (bf16[256,1024]{1,0:T(8,128)(2,1)}, bf16[256,1024]{1,0:T(8,128)(2,1)}, u32[]{:S(2)}, u32[]{:S(2)}) collective-permute-start(bf16[256,1024]{1,0:T(8,128)(2,1)} %get-tuple-element.13), channel_id=1, source_target_pairs={{0,128},{64,192},{128,0},{192,64},{1,129},{65,193},{129,1},{193,65... | collective-permute-start | bytes 1572872 | tf_op jit(solution)/shard_map/ppermute | solution.py:20
  31.6 99.9 %collective-permute-start.3 = (bf16[256,1024]{1,0:T(8,128)(2,1)}, bf16[256,1024]{1,0:T(8,128)(2,1)}, u32[]{:S(2)}, u32[]{:S(2)}) collective-permute-start(bf16[256,1024]{1,0:T(8,128)(2,1)} %get-tuple-element.11), channel_id=1, source_target_pairs={{0,64},{64,128},{128,192},{192,0},{1,65},{65,129},{129,193},{193,1... | collective-permute-start | bytes 1572872 | tf_op jit(solution)/shard_map/ppermute | solution.py:20
  32.9 88.2 %copy-start.2 = (bf16[512,128]{1,0:T(8,128)(2,1)S(1)}, bf16[512,128]{1,0:T(8,128)(2,1)}, u32[]{:S(2)}) copy-start(bf16[512,128]{1,0:T(8,128)(2,1)} %param.8) | copy-start | bytes 393220
  35.1 86.1 %copy-start.3 = (bf16[512,128]{1,0:T(8,128)(2,1)S(1)}, bf16[512,128]{1,0:T(8,128)(2,1)}, u32[]{:S(2)}) copy-start(bf16[512,128]{1,0:T(8,128)(2,1)} %param.7) | copy-start | bytes 393220
  134.1 36.8 %collective-permute-start.6 = (bf16[3,256,1024]{2,1,0:T(8,128)(2,1)}, bf16[3,256,1024]{2,1,0:T(8,128)(2,1)}, u32[]{:S(2)}, u32[]{:S(2)}) collective-permute-start(bf16[3,256,1024]{2,1,0:T(8,128)(2,1)} %pad_maximum_fusion), channel_id=1, source_target_pairs={{0,1},{1,0},{2,3},{3,2},{4,5},{5,4},{6,7},{7,6},{8,9},{9,8},{10,11... | collective-permute-start | bytes 4718600 | tf_op jit(solution)/shard_map/ppermute | solution.py:20
  142.2 0.7 copy-start.4
  142.2 0.7 copy-start.5
  142.2 7.6 %slice-start = ((s8[6291456]{0:T(1024)(128)(4,1)}), s8[4194304]{0:T(1024)(128)(4,1)S(1)}, s32[]{:S(2)}) async-start(s8[6291456]{0:T(1024)(128)(4,1)} %bitcast.168), calls=%async_computation.1 | async-start | bytes 8388608
  142.9 6.9 %slice-start.1 = ((s8[6291456]{0:T(1024)(128)(4,1)}), s8[2097152]{0:T(1024)(128)(4,1)S(1)}, s32[]{:S(2)}) async-start(s8[6291456]{0:T(1024)(128)(4,1)} %bitcast.168), calls=%async_computation.2 | async-start | bytes 4194304
  154.8 14.6 %collective-permute-start.7 = (bf16[512,512]{0,1:T(8,128)(2,1)S(1)}, bf16[512,512]{0,1:T(8,128)(2,1)S(1)}, u32[]{:S(2)}, u32[]{:S(2)}) collective-permute-start(bf16[512,512]{0,1:T(8,128)(2,1)S(1)} %bitcast.171), channel_id=1, source_target_pairs={{0,128},{64,192},{128,0},{192,64},{1,129},{65,193},{129,1},{193,65... | collective-permute-start | bytes 1572872 | tf_op jit(solution)/shard_map/ppermute | solution.py:20
  155.1 29.4 %collective-permute-start.8 = (bf16[512,512]{0,1:T(8,128)(2,1)S(1)}, bf16[512,512]{0,1:T(8,128)(2,1)S(1)}, u32[]{:S(2)}, u32[]{:S(2)}) collective-permute-start(bf16[512,512]{0,1:T(8,128)(2,1)S(1)} %bitcast.172), channel_id=1, source_target_pairs={{0,192},{64,0},{128,64},{192,128},{1,193},{65,1},{129,65},{193,129... | collective-permute-start | bytes 1572872 | tf_op jit(solution)/shard_map/ppermute | solution.py:20
  157.0 24.5 %collective-permute-start.2 = (bf16[512,512]{0,1:T(8,128)(2,1)S(1)}, bf16[512,512]{0,1:T(8,128)(2,1)S(1)}, u32[]{:S(2)}, u32[]{:S(2)}) collective-permute-start(bf16[512,512]{0,1:T(8,128)(2,1)S(1)} %bitcast.173), channel_id=1, source_target_pairs={{0,64},{64,128},{128,192},{192,0},{1,65},{65,129},{129,193},{193,1... | collective-permute-start | bytes 1572872 | tf_op jit(solution)/shard_map/ppermute | solution.py:20
  186.0 2.8 %copy-start.1 = (bf16[512,512]{1,0:T(8,128)(2,1)S(1)}, bf16[512,512]{1,0:T(8,128)(2,1)}, u32[]{:S(2)}) copy-start(bf16[512,512]{1,0:T(8,128)(2,1)} %param.6) | copy-start | bytes 1572868
